TPU v7x, 32 devices: a whole 2x2x4 slice. The times are simulated.
32 devices in a mesh: row: 4 (over y, x), col: 8 (over z, core).
Axes of the slice: x: 2, y: 2, z: 4, core: 2. Of those that a mesh axis runs over, the one named last changes fastest.
Arguments:
- frames: bfloat16 [4096, 440], P('col'), may hold values from -6 to 6
- center_picks: int32 [8, 8, 64], P('col'), may hold values from 0 to 511, as said below
- send_counts: int32 [8, 8], P(None, 'col'), may hold values from 0 to 64, as said below
- send_offsets: int32 [8, 8], P(None, 'col'), may hold values from 0 to 256, as said below
Outputs:
- factor_panels: float32 [4, 512, 1024], P('row', 'col')
- trailing: float32 [4, 512, 8, 256], P('row', None, 'col')
Inputs may be any that keep to these rules, and one draw needn't show every extreme that they name: `center_picks`: for each owner the entries over all destinations and slots are distinct local frame indices. `send_counts`: for each destination the counts over owners sum to 256; every destination has an owner that fills all 64 slots and one that sends nothing. `send_offsets`: for each destination the owners' segments [offset, offset + count) cover 0 to 255 without intersection, in an order that varies by destination; an owner that sends nothing may start at 256.
All inputs are finite; a program needn't handle non-finite values.
Results may differ from a plain program's by a relative error of at most 0.0003.
Values may be sent and summed in bfloat16 or wider, within the bound.
No kernel may reach another device: no remote copies, remote signals or barrier semaphores. Data moves between devices by JAX's collectives and lax.ppermute only.
A program may use at most 128 MiB of HBM per device.

v0:
```python
import jax
import jax.numpy as jnp
from jax import lax
from jax.sharding import PartitionSpec as P

PANEL = 256
PANELS = 4
CENT_DEV = 256


kernel_scale = 0.6
ridge_shift = 0.1


def spread(value, axis, source):
    kept = jnp.where(lax.axis_index(axis) == source, value, 0).astype(value.dtype)
    return lax.psum(kept, axis)


def gaussian(left_feats, right_feats):
    inner = lax.dot_general(
        left_feats, right_feats, (((1,), (1,)), ((), ())), preferred_element_type=jnp.float32
    )
    left_norm = jnp.sum(jnp.square(left_feats.astype(jnp.float32)), axis=1)
    right_norm = jnp.sum(jnp.square(right_feats.astype(jnp.float32)), axis=1)
    feat_width = left_feats.shape[1]
    return jnp.exp(
        -(kernel_scale / feat_width) * (left_norm[:, None] + right_norm[None, :] - 2.0 * inner)
    )


def outer_minus(column, panel_cols, rows_piece):
    return column - lax.dot_general(
        panel_cols,
        rows_piece,
        (((1,), (1,)), ((), ())),
        precision=lax.Precision.HIGHEST,
        preferred_element_type=jnp.float32,
    )


def make_panel(column, factor, row_tile, panel_step):
    solved = jax.scipy.linalg.solve_triangular(factor, column.T, lower=True).T
    repeated = jnp.tile(factor, (column.shape[0] // factor.shape[0], 1))
    return jnp.where(
        (row_tile > panel_step)[:, None],
        solved,
        jnp.where((row_tile == panel_step)[:, None], repeated, jnp.zeros_like(solved)),
    )


def update_slots(columns, panel_cols, col_rows):
    columns[0] = outer_minus(columns[0], panel_cols, col_rows)
    return columns


def per_device(frames, center_picks, send_counts, send_offsets):
    rows_axis = lax.axis_size("row")
    cols_axis = lax.axis_size("col")
    row_id = lax.axis_index("row")
    col_id = lax.axis_index("col")
    feat_width = frames.shape[1]
    capacity = center_picks.shape[2]
    outgoing = frames[center_picks[0]]
    incoming = lax.all_to_all(outgoing, "col", split_axis=0, concat_axis=0, tiled=True)
    position = jnp.arange(CENT_DEV, dtype=jnp.int32)
    starts = send_offsets[:, 0]
    lengths = send_counts[:, 0]
    inside = (position[:, None] >= starts[None, :]) & (
        position[:, None] < (starts + lengths)[None, :]
    )
    source = jnp.sum(jnp.where(inside, jnp.arange(cols_axis, dtype=jnp.int32)[None, :], 0), axis=1)
    within = position - jnp.sum(jnp.where(inside, starts[None, :], 0), axis=1)
    own_feats = incoming.reshape(cols_axis * capacity, feat_width)[source * capacity + within]
    col_slots = CENT_DEV // PANEL
    row_tiles_dev = col_slots * cols_axis // rows_axis
    rows_dev = row_tiles_dev * PANEL
    tile_range = jnp.arange(row_tiles_dev, dtype=jnp.int32)
    gathered = lax.all_gather(own_feats, "col", axis=0, tiled=True)
    blocks = gathered.reshape(cols_axis, col_slots, PANEL, feat_width)
    my_tiles = row_id + rows_axis * tile_range
    row_feats = blocks[my_tiles % cols_axis, my_tiles // cols_axis].reshape(rows_dev, feat_width)
    local_rows = jnp.arange(rows_dev, dtype=jnp.int32)
    row_tile = row_id + rows_axis * (local_rows // PANEL)
    global_row = row_tile * PANEL + local_rows % PANEL
    local_cols = jnp.arange(CENT_DEV, dtype=jnp.int32)
    global_col = (col_id + cols_axis * (local_cols // PANEL)) * PANEL + local_cols % PANEL
    kernel = gaussian(row_feats, own_feats) + ridge_shift * (
        global_row[:, None] == global_col[None, :]
    ).astype(jnp.float32)
    columns = [kernel]
    panels = []
    for panel_step in range(PANELS):
        slot_now = panel_step // cols_axis
        tile_slot = panel_step // rows_axis
        diag_here = columns[slot_now][tile_slot * PANEL : (tile_slot + 1) * PANEL]
        diag_block = spread(diag_here, "row", panel_step % rows_axis)
        factor = jnp.linalg.cholesky(diag_block)
        panel_here = make_panel(columns[slot_now], factor, row_tile, panel_step)
        panel_cols = spread(panel_here, "col", panel_step % cols_axis)
        here_rows = lax.dynamic_slice_in_dim(
            panel_cols, (col_id + 0) // rows_axis * PANEL, PANEL, 0
        )
        col_rows = spread(here_rows, "row", col_id % rows_axis)
        panels.append(panel_cols)
        columns = update_slots(columns, panel_cols, col_rows)
    trailing = columns[0].reshape(1, rows_dev, 1, CENT_DEV)
    every_panel = jnp.concatenate(panels, axis=1)
    share_rows = rows_dev // cols_axis
    panel_share = lax.dynamic_slice_in_dim(every_panel, col_id * share_rows, share_rows, 0).reshape(
        1, share_rows, PANELS * PANEL
    )
    return (panel_share, trailing)


def solution(mesh):
    in_specs = (P("col", None), P("col", None, None), P(None, "col"), P(None, "col"))
    out_specs = (P("row", "col", None), P("row", None, "col", None))
    return jax.shard_map(
        per_device, mesh=mesh, in_specs=in_specs, out_specs=out_specs, check_vma=False
    )
```

profile of v0, /device:TPU:0, one launch (start us, length us, event | category | flops | bytes accessed | tf_op | source)
XLA Modules:
  0.0 926.7 jit_solution(15417714206202597751)
XLA Ops:
  9.2 2.6 gather_fusion
  11.8 6.3 all-to-all-start
  18.3 15.2 %all-to-all-done = bf16[8,64,440]{2,1,0:T(8,128)(2,1)S(1)} async-done(((bf16[8,64,440]{2,1,0:T(8,128)(2,1)}), bf16[8,64,440]{2,1,0:T(8,128)(2,1)S(1)}, u32[]{:S(2)}, u32[]{:S(2)}) %all-to-all-start) | async-done | bytes 450592 | tf_op jit(solution)/shard_map/all_to_all | solution.py:65
  33.5 1.9 gather_fusion.1
  36.6 27.0 %all-gather.3.cloned.1.call-done = bf16[2048,440]{1,0:T(8,128)(2,1)} async-done(((bf16[256,440]{1,0:T(8,128)(2,1)}), bf16[2048,440]{1,0:T(8,128)(2,1)}) %all-gather.3.cloned.1.call-update) | async-done | bytes 1802256 | tf_op jit(solution)/shard_map/all_gather | solution.py:79
  63.5 2.2 gather_fusion.2
  67.6 42.3 %all-reduce.14.cloned.1.call-done = f32[256,256]{0,1:T(8,128)} async-done(((f32[256,256]{0,1:T(8,128)}), f32[256,256]{0,1:T(8,128)}) %all-reduce.14.cloned.1.call-update) | async-done | bytes 262160 | tf_op jit(solution)/shard_map/psum | solution.py:17
  112.0 11.7 %cholesky.214 = f32[128,128]{1,0:T(8,128)S(1)} custom-call(f32[128,128]{1,0:T(8,128)S(1)} %cholesky.346), custom_call_target="Cholesky" | custom-call | tf_op jit(solution)/shard_map/jit(cholesky)/cholesky | solution.py:98
  123.7 9.8 %custom-call.19 = f32[1,128,128]{1,2,0:T(8,128)S(1)} custom-call(f32[1,128,128]{2,1,0:T(8,128)S(1)} %get-tuple-element.105), custom_call_target="InvertDiagBlocksLowerTriangular" | custom-call | tf_op jit(solution)/shard_map/jit(cholesky)/cholesky | solution.py:98
  134.0 11.7 %cholesky.231 = f32[128,128]{1,0:T(8,128)S(1)} custom-call(f32[128,128]{1,0:T(8,128)S(1)} %convolution_subtract_fusion.8), custom_call_target="Cholesky" | custom-call | tf_op jit(solution)/shard_map/jit(cholesky)/cholesky | solution.py:98
  148.0 4.6 while.8
  152.6 19.7 %custom-call.20 = f32[2,128,128]{1,2,0:T(8,128)S(1)} custom-call(f32[2,128,128]{2,1,0:T(8,128)S(1)} %get-tuple-element.30), custom_call_target="InvertDiagBlocksLowerTriangular" | custom-call | tf_op jit(solution)/shard_map/jit(_solve_triangular)/triangular_solve | solution.py:43
  174.8 56.2 %all-reduce.16.cloned.1.call-done = f32[512,256]{0,1:T(8,128)} async-done(((f32[512,256]{0,1:T(8,128)}), f32[512,256]{0,1:T(8,128)}) %all-reduce.16.cloned.1.call-update) | async-done | bytes 524304 | tf_op jit(solution)/shard_map/psum | solution.py:17
  231.1 1.7 dynamic-slice_select_fusion.3
  232.8 43.5 %all-reduce.18.cloned.1.call-done = f32[256,256]{0,1:T(8,128)} async-done(((f32[256,256]{0,1:T(8,128)}), f32[256,256]{0,1:T(8,128)}) %all-reduce.18.cloned.1.call-update) | async-done | bytes 262160 | tf_op jit(solution)/shard_map/psum | solution.py:17
  276.4 1.8 bitcast_subtract_fusion.2
  279.2 43.7 %all-reduce.20.cloned.1.call-done = f32[256,256]{0,1:T(8,128)} async-done(((f32[256,256]{0,1:T(8,128)}), f32[256,256]{0,1:T(8,128)}) %all-reduce.20.cloned.1.call-update) | async-done | bytes 262160 | tf_op jit(solution)/shard_map/psum | solution.py:17
  325.0 11.7 %cholesky.248 = f32[128,128]{1,0:T(8,128)S(1)} custom-call(f32[128,128]{1,0:T(8,128)S(1)} %cholesky.349), custom_call_target="Cholesky" | custom-call | tf_op jit(solution)/shard_map/jit(cholesky)/cholesky | solution.py:98
  336.8 9.8 %custom-call.21 = f32[1,128,128]{1,2,0:T(8,128)S(1)} custom-call(f32[1,128,128]{2,1,0:T(8,128)S(1)} %get-tuple-element.101), custom_call_target="InvertDiagBlocksLowerTriangular" | custom-call | tf_op jit(solution)/shard_map/jit(cholesky)/cholesky | solution.py:98
  347.1 11.7 %cholesky.265 = f32[128,128]{1,0:T(8,128)S(1)} custom-call(f32[128,128]{1,0:T(8,128)S(1)} %convolution_subtract_fusion.7), custom_call_target="Cholesky" | custom-call | tf_op jit(solution)/shard_map/jit(cholesky)/cholesky | solution.py:98
  361.6 4.3 while.9
  365.9 19.7 %custom-call.22 = f32[2,128,128]{1,2,0:T(8,128)S(1)} custom-call(f32[2,128,128]{2,1,0:T(8,128)S(1)} %get-tuple-element.31), custom_call_target="InvertDiagBlocksLowerTriangular" | custom-call | tf_op jit(solution)/shard_map/jit(_solve_triangular)/triangular_solve | solution.py:43
  388.2 56.2 %all-reduce.22.cloned.1.call-done = f32[512,256]{0,1:T(8,128)} async-done(((f32[512,256]{0,1:T(8,128)}), f32[512,256]{0,1:T(8,128)}) %all-reduce.22.cloned.1.call-update) | async-done | bytes 524304 | tf_op jit(solution)/shard_map/psum | solution.py:17
  444.4 1.7 dynamic-slice_select_fusion.2
  446.2 43.9 %all-reduce.24.cloned.1.call-done = f32[256,256]{0,1:T(8,128)} async-done(((f32[256,256]{0,1:T(8,128)}), f32[256,256]{0,1:T(8,128)}) %all-reduce.24.cloned.1.call-update) | async-done | bytes 262160 | tf_op jit(solution)/shard_map/psum | solution.py:17
  490.1 1.8 bitcast_subtract_fusion.1
  492.8 43.8 %all-reduce.26.cloned.1.call-done = f32[256,256]{0,1:T(8,128)} async-done(((f32[256,256]{0,1:T(8,128)}), f32[256,256]{0,1:T(8,128)}) %all-reduce.26.cloned.1.call-update) | async-done | bytes 262160 | tf_op jit(solution)/shard_map/psum | solution.py:17
  538.6 11.7 %cholesky.282 = f32[128,128]{1,0:T(8,128)S(1)} custom-call(f32[128,128]{1,0:T(8,128)S(1)} %cholesky.352), custom_call_target="Cholesky" | custom-call | tf_op jit(solution)/shard_map/jit(cholesky)/cholesky | solution.py:98
  550.4 9.8 %custom-call.23 = f32[1,128,128]{1,2,0:T(8,128)S(1)} custom-call(f32[1,128,128]{2,1,0:T(8,128)S(1)} %get-tuple-element.97), custom_call_target="InvertDiagBlocksLowerTriangular" | custom-call | tf_op jit(solution)/shard_map/jit(cholesky)/cholesky | solution.py:98
  560.7 11.7 %cholesky.299 = f32[128,128]{1,0:T(8,128)S(1)} custom-call(f32[128,128]{1,0:T(8,128)S(1)} %convolution_subtract_fusion.6), custom_call_target="Cholesky" | custom-call | tf_op jit(solution)/shard_map/jit(cholesky)/cholesky | solution.py:98
  575.2 4.3 while.10
  576.1 1.4 bitcast_dynamic-update-slice_fusion.10
  578.1 1.4 bitcast_dynamic-update-slice_fusion.10
  579.5 19.7 %custom-call.24 = f32[2,128,128]{1,2,0:T(8,128)S(1)} custom-call(f32[2,128,128]{2,1,0:T(8,128)S(1)} %get-tuple-element.32), custom_call_target="InvertDiagBlocksLowerTriangular" | custom-call | tf_op jit(solution)/shard_map/jit(_solve_triangular)/triangular_solve | solution.py:43
  601.8 56.3 %all-reduce.28.cloned.1.call-done = f32[512,256]{0,1:T(8,128)} async-done(((f32[512,256]{0,1:T(8,128)}), f32[512,256]{0,1:T(8,128)}) %all-reduce.28.cloned.1.call-update) | async-done | bytes 524304 | tf_op jit(solution)/shard_map/psum | solution.py:17
  658.1 1.7 dynamic-slice_select_fusion.1
  659.8 43.5 %all-reduce.30.cloned.1.call-done = f32[256,256]{0,1:T(8,128)} async-done(((f32[256,256]{0,1:T(8,128)}), f32[256,256]{0,1:T(8,128)}) %all-reduce.30.cloned.1.call-update) | async-done | bytes 262160 | tf_op jit(solution)/shard_map/psum | solution.py:17
  703.4 1.8 bitcast_subtract_fusion
  706.0 44.0 %all-reduce.32.cloned.1.call-done = f32[256,256]{0,1:T(8,128)} async-done(((f32[256,256]{0,1:T(8,128)}), f32[256,256]{0,1:T(8,128)}) %all-reduce.32.cloned.1.call-update) | async-done | bytes 262160 | tf_op jit(solution)/shard_map/psum | solution.py:17
  752.2 11.7 %cholesky.316 = f32[128,128]{1,0:T(8,128)S(1)} custom-call(f32[128,128]{1,0:T(8,128)S(1)} %cholesky.355), custom_call_target="Cholesky" | custom-call | tf_op jit(solution)/shard_map/jit(cholesky)/cholesky | solution.py:98
  763.9 9.8 %custom-call.25 = f32[1,128,128]{1,2,0:T(8,128)S(1)} custom-call(f32[1,128,128]{2,1,0:T(8,128)S(1)} %get-tuple-element.93), custom_call_target="InvertDiagBlocksLowerTriangular" | custom-call | tf_op jit(solution)/shard_map/jit(cholesky)/cholesky | solution.py:98
  774.2 11.7 %cholesky.333 = f32[128,128]{1,0:T(8,128)S(1)} custom-call(f32[128,128]{1,0:T(8,128)S(1)} %convolution_subtract_fusion.5), custom_call_target="Cholesky" | custom-call | tf_op jit(solution)/shard_map/jit(cholesky)/cholesky | solution.py:98
  788.6 4.2 while.11
  792.8 19.7 %custom-call.26 = f32[2,128,128]{1,2,0:T(8,128)S(1)} custom-call(f32[2,128,128]{2,1,0:T(8,128)S(1)} %get-tuple-element.33), custom_call_target="InvertDiagBlocksLowerTriangular" | custom-call | tf_op jit(solution)/shard_map/jit(_solve_triangular)/triangular_solve | solution.py:43
  815.1 56.3 %all-reduce.34.cloned.1.call-done = f32[512,256]{0,1:T(8,128)} async-done(((f32[512,256]{0,1:T(8,128)}), f32[512,256]{0,1:T(8,128)}) %all-reduce.34.cloned.1.call-update) | async-done | bytes 524304 | tf_op jit(solution)/shard_map/psum | solution.py:17
  871.4 1.7 dynamic-slice_select_fusion
  875.2 41.9 %all-reduce.36.cloned.1.call-done = f32[256,256]{0,1:T(8,128)} async-done(((f32[256,256]{0,1:T(8,128)}), f32[256,256]{0,1:T(8,128)}) %all-reduce.36.cloned.1.call-update) | async-done | bytes 262160 | tf_op jit(solution)/shard_map/psum | solution.py:17
  917.0 1.6 fusion
  (170 shorter events, 49.9 us)
Async XLA Ops:
  9.2 9.0 copy-start.5
  9.2 9.0 copy-start.6
  11.8 21.7 %all-to-all-start = ((bf16[8,64,440]{2,1,0:T(8,128)(2,1)}), bf16[8,64,440]{2,1,0:T(8,128)(2,1)S(1)}, u32[]{:S(2)}, u32[]{:S(2)}) async-start(bf16[8,64,440]{2,1,0:T(8,128)(2,1)} %bitcast.1), calls=%async_computation | async-start | bytes 1048576 | tf_op jit(solution)/shard_map/all_to_all | solution.py:65
  18.1 45.4 %all-gather.3.cloned.1.call-start = ((), (), s32[]{:S(2)}) async-start(), calls=%async_computation.13 | async-start | bytes 2359296 | tf_op jit(solution)/shard_map/all_gather | solution.py:79
  35.3 30.6 %copy-start.4 = (bf16[256,440]{1,0:T(8,128)(2,1)S(1)}, bf16[256,440]{1,0:T(8,128)(2,1)}, u32[]{:S(2)}) copy-start(bf16[256,440]{1,0:T(8,128)(2,1)} %gather_fusion.1) | copy-start | bytes 675844
  35.4 74.5 %all-reduce.14.cloned.1.call-start = ((), (), s32[]{:S(2)}) async-start(), calls=%async_computation.1 | async-start | bytes 524288 | tf_op jit(solution)/shard_map/psum | solution.py:17
  67.3 163.8 %all-reduce.16.cloned.1.call-start = ((), (), s32[]{:S(2)}) async-start(), calls=%async_computation.2 | async-start | bytes 1048576 | tf_op jit(solution)/shard_map/psum | solution.py:17
  174.8 101.6 %all-reduce.18.cloned.1.call-start = ((), (), s32[]{:S(2)}) async-start(), calls=%async_computation.3 | async-start | bytes 524288 | tf_op jit(solution)/shard_map/psum | solution.py:17
  232.8 90.2 %all-reduce.20.cloned.1.call-start = ((), (), s32[]{:S(2)}) async-start(), calls=%async_computation.4 | async-start | bytes 524288 | tf_op jit(solution)/shard_map/psum | solution.py:17
  279.1 165.3 %all-reduce.22.cloned.1.call-start = ((), (), s32[]{:S(2)}) async-start(), calls=%async_computation.5 | async-start | bytes 1048576 | tf_op jit(solution)/shard_map/psum | solution.py:17
  388.1 102.0 %all-reduce.24.cloned.1.call-start = ((), (), s32[]{:S(2)}) async-start(), calls=%async_computation.6 | async-start | bytes 524288 | tf_op jit(solution)/shard_map/psum | solution.py:17
  446.1 90.5 %all-reduce.26.cloned.1.call-start = ((), (), s32[]{:S(2)}) async-start(), calls=%async_computation.7 | async-start | bytes 524288 | tf_op jit(solution)/shard_map/psum | solution.py:17
  492.7 165.4 %all-reduce.28.cloned.1.call-start = ((), (), s32[]{:S(2)}) async-start(), calls=%async_computation.8 | async-start | bytes 1048576 | tf_op jit(solution)/shard_map/psum | solution.py:17
  601.8 101.6 %all-reduce.30.cloned.1.call-start = ((), (), s32[]{:S(2)}) async-start(), calls=%async_computation.9 | async-start | bytes 524288 | tf_op jit(solution)/shard_map/psum | solution.py:17
  659.8 90.3 %all-reduce.32.cloned.1.call-start = ((), (), s32[]{:S(2)}) async-start(), calls=%async_computation.10 | async-start | bytes 524288 | tf_op jit(solution)/shard_map/psum | solution.py:17
  706.0 165.4 %all-reduce.34.cloned.1.call-start = ((), (), s32[]{:S(2)}) async-start(), calls=%async_computation.11 | async-start | bytes 1048576 | tf_op jit(solution)/shard_map/psum | solution.py:17
  814.0 59.1 %copy-start.1 = (f32[512,256]{0,1:T(8,128)S(1)}, f32[512,256]{0,1:T(8,128)}, u32[]{:S(2)}) copy-start(f32[512,256]{0,1:T(8,128)} %all-reduce.16.cloned.1.call-done) | copy-start | bytes 1572868
  814.0 59.1 %copy-start.2 = (f32[512,256]{0,1:T(8,128)S(1)}, f32[512,256]{0,1:T(8,128)}, u32[]{:S(2)}) copy-start(f32[512,256]{0,1:T(8,128)} %all-reduce.22.cloned.1.call-done) | copy-start | bytes 1572868
  814.0 59.1 %copy-start.3 = (f32[512,256]{0,1:T(8,128)S(1)}, f32[512,256]{0,1:T(8,128)}, u32[]{:S(2)}) copy-start(f32[512,256]{0,1:T(8,128)} %all-reduce.28.cloned.1.call-done) | copy-start | bytes 1572868
  815.0 102.0 %all-reduce.36.cloned.1.call-start = ((), (), s32[]{:S(2)}) async-start(), calls=%async_computation.12 | async-start | bytes 524288 | tf_op jit(solution)/shard_map/psum | solution.py:17
  871.4 45.7 %copy-start = (f32[512,256]{0,1:T(8,128)S(1)}, f32[512,256]{0,1:T(8,128)}, u32[]{:S(2)}) copy-start(f32[512,256]{0,1:T(8,128)} %all-reduce.34.cloned.1.call-done) | copy-start | bytes 1572868
Sparse Core Ops, SparseCore 0:
  35.5 27.9 all-gather.2
  67.4 42.4 all-reduce.13
  174.9 56.1 all-reduce.15
  234.4 41.8 all-reduce.17
  280.0 42.9 all-reduce.19
  388.2 56.1 all-reduce.21
  448.2 41.8 all-reduce.23
  493.6 42.9 all-reduce.25
  601.9 56.1 all-reduce.27
  661.4 41.9 all-reduce.29
  707.1 42.9 all-reduce.31
  815.1 56.1 all-reduce.33
  875.1 41.8 all-reduce.35
where the time goes:
time: 930 us; the launch traced here: 927 us
  waiting for transfers between devices  614 us (66%)
  other arithmetic  238 us (26%)
  local copies, waits for them, and re-layouts  31.9 us (3%)
  between operations  20.4 us (2%)
  matrix products  14 us (2%)
    psum x12, waiting for transfers between devices, spread(): return lax.psum(kept, axis)  572 us
    another operation x27, other arithmetic, per_device(): factor = jnp.linalg.cholesky(diag_block)  138 us
    another operation x9, other arithmetic, make_panel(): solved = jax.scipy.linalg.solve_triangular(factor, column.T, lower=True).T  78.8 us
    all_gather x1, waiting for transfers between devices, per_device(): gathered = lax.all_gather(own_feats, 'col', axis=0, tiled=True)  27 us
  transfers between devices with their start and end apart: 14, of which 14 were waited for; matrix products, arithmetic and copies ran while one was open for 0% of the time, Pallas kernels for 0%

commit v1 on v0

v1 whole, which is shorter than its diff:
```python
import jax
import jax.numpy as jnp
from jax import lax
from jax.sharding import PartitionSpec as P

PANEL = 256
PANELS = 4
CENT_DEV = 256


kernel_scale = 0.6
ridge_shift = 0.1


def gaussian(left_feats, right_feats):
    inner = lax.dot_general(
        left_feats, right_feats, (((1,), (1,)), ((), ())), preferred_element_type=jnp.float32
    )
    left_norm = jnp.sum(jnp.square(left_feats.astype(jnp.float32)), axis=1)
    right_norm = jnp.sum(jnp.square(right_feats.astype(jnp.float32)), axis=1)
    feat_width = left_feats.shape[1]
    return jnp.exp(
        -(kernel_scale / feat_width) * (left_norm[:, None] + right_norm[None, :] - 2.0 * inner)
    )


def ridged(left_feats, left_index, right_feats, right_index):
    eye = (left_index[:, None] == right_index[None, :]).astype(jnp.float32)
    return gaussian(left_feats, right_feats) + ridge_shift * eye


def matmul_t(left, right):
    return lax.dot_general(
        left,
        right,
        (((1,), (1,)), ((), ())),
        precision=lax.Precision.HIGHEST,
        preferred_element_type=jnp.float32,
    )


def tile_rows(tiles):
    return (tiles[:, None] * PANEL + jnp.arange(PANEL, dtype=jnp.int32)[None, :]).reshape(-1)


def per_device(frames, center_picks, send_counts, send_offsets):
    rows_axis = lax.axis_size("row")
    cols_axis = lax.axis_size("col")
    row_id = lax.axis_index("row")
    col_id = lax.axis_index("col")
    feat_width = frames.shape[1]
    capacity = center_picks.shape[2]
    outgoing = frames[center_picks[0]]
    incoming = lax.all_to_all(outgoing, "col", split_axis=0, concat_axis=0, tiled=True)
    position = jnp.arange(CENT_DEV, dtype=jnp.int32)
    starts = send_offsets[:, 0]
    lengths = send_counts[:, 0]
    inside = (position[:, None] >= starts[None, :]) & (
        position[:, None] < (starts + lengths)[None, :]
    )
    source = jnp.sum(jnp.where(inside, jnp.arange(cols_axis, dtype=jnp.int32)[None, :], 0), axis=1)
    within = position - jnp.sum(jnp.where(inside, starts[None, :], 0), axis=1)
    own_feats = incoming.reshape(cols_axis * capacity, feat_width)[source * capacity + within]
    col_slots = CENT_DEV // PANEL
    row_tiles_dev = col_slots * cols_axis // rows_axis
    gathered = lax.all_gather(own_feats, "col", axis=0, tiled=True)
    centers = (
        gathered.reshape(cols_axis, col_slots, PANEL, feat_width)
        .transpose(1, 0, 2, 3)
        .reshape(cols_axis * col_slots * PANEL, feat_width)
    )
    panel_tiles = jnp.arange(PANELS, dtype=jnp.int32)
    my_row_tiles = row_id + rows_axis * jnp.arange(row_tiles_dev, dtype=jnp.int32)
    my_col_tiles = col_id + cols_axis * jnp.arange(col_slots, dtype=jnp.int32)
    ext_tiles = jnp.concatenate([panel_tiles, my_row_tiles, my_col_tiles])
    ext_index = tile_rows(ext_tiles)
    panel_index = tile_rows(panel_tiles)
    ext_feats = centers[ext_index]
    panel_feats = centers[:PANELS * PANEL]
    kernel = ridged(ext_feats, ext_index, panel_feats, panel_index)
    ext_tile = ext_index // PANEL
    columns = [kernel[:, q * PANEL : (q + 1) * PANEL] for q in range(PANELS)]
    panels = []
    for panel_step in range(PANELS):
        column = columns[panel_step]
        diag_block = column[panel_step * PANEL : (panel_step + 1) * PANEL]
        factor = jnp.linalg.cholesky(diag_block)
        solved = lax.linalg.triangular_solve(
            factor, column, left_side=False, lower=True, transpose_a=True
        )
        repeated = jnp.tile(factor, (column.shape[0] // PANEL, 1))
        panel = jnp.where(
            (ext_tile > panel_step)[:, None],
            solved,
            jnp.where((ext_tile == panel_step)[:, None], repeated, jnp.zeros_like(solved)),
        )
        panels.append(panel)
        for later in range(panel_step + 1, PANELS):
            columns[later] = columns[later] - matmul_t(
                panel, panel[later * PANEL : (later + 1) * PANEL]
            )
    every_panel = jnp.concatenate(panels, axis=1)
    base = PANELS * PANEL
    rows_dev = row_tiles_dev * PANEL
    row_panel = every_panel[base : base + rows_dev]
    col_panel = every_panel[base + rows_dev :]
    row_index = ext_index[base : base + rows_dev]
    col_index = ext_index[base + rows_dev :]
    block = ridged(ext_feats[base : base + rows_dev], row_index, ext_feats[base + rows_dev :], col_index)
    trailing = (block - matmul_t(row_panel, col_panel)).reshape(1, rows_dev, 1, CENT_DEV)
    share_rows = rows_dev // cols_axis
    panel_share = lax.dynamic_slice_in_dim(row_panel, col_id * share_rows, share_rows, 0).reshape(
        1, share_rows, PANELS * PANEL
    )
    return (panel_share, trailing)


def solution(mesh):
    in_specs = (P("col", None), P("col", None, None), P(None, "col"), P(None, "col"))
    out_specs = (P("row", "col", None), P("row", None, "col", None))
    return jax.shard_map(
        per_device, mesh=mesh, in_specs=in_specs, out_specs=out_specs, check_vma=False
    )
```

time: 930 us -> 412 us (0.44)
  waiting for transfers between devices: 614 us -> 42.9 us
  matrix products: 14 us -> 51.3 us
  local copies, waits for them, and re-layouts: 31.9 us -> 54.7 us
    psum x12 -> x0, waiting for transfers between devices: 572 us -> none  [spread(): return lax.psum(kept, axis)]
    another operation x12, matrix products: 4.82 us -> 21.4 us  [per_device(): lax.linalg.triangular_solve(factor, column, left_side=False, lower=True,...]
    dot_general x4 -> x7, matrix products: 6.9 us -> 23.4 us  [matmul_t(): lax.dot_general(left, right, (((1,), (1,)), ((), ())), precision=lax.Prec...]
    another operation x33 -> x37, local copies, waits for them, and re-layouts: 16.9 us -> 31 us  [the longest x29 15.9 us: per_device(): lax.linalg.triangular_solve(factor, column, left_side=False, lower=True,...]
  transfers between devices with their start and end apart: 14 -> 2, of which waited for: 14 -> 2; matrix products, arithmetic and copies ran while one was open for 0% -> 0% of each run, Pallas kernels for 0% -> 0%
where the time goes in v1:
time: 412 us; the launch traced here: 408 us
  other arithmetic  232 us (56%)
  local copies, waits for them, and re-layouts  54.7 us (13%)
  matrix products  51.3 us (12%)
  waiting for transfers between devices  42.9 us (10%)
  between operations  20.2 us (5%)
  starting transfers between devices  6.36 us (2%)
    another operation x27, other arithmetic, per_device(): factor = jnp.linalg.cholesky(diag_block)  138 us
    another operation x9, other arithmetic, per_device(): lax.linalg.triangular_solve(factor, column, left_side=False, lower=True,...  78.8 us
    all_gather x1, waiting for transfers between devices, per_device(): gathered = lax.all_gather(own_feats, 'col', axis=0, tiled=True)  27.8 us
    dot_general x7, matrix products, matmul_t(): lax.dot_general(left, right, (((1,), (1,)), ((), ())), precision=lax.Prec...  23.4 us
    another operation x12, matrix products, per_device(): lax.linalg.triangular_solve(factor, column, left_side=False, lower=True,...  21.4 us
    another operation x29, local copies, waits for them, and re-layouts, per_device(): lax.linalg.triangular_solve(factor, column, left_side=False, lower=True,...  15.9 us
    all_to_all x1, waiting for transfers between devices, per_device(): lax.all_to_all(outgoing, 'col', split_axis=0, concat_axis=0, tiled=True)  15.2 us
    another operation x8, local copies, waits for them, and re-layouts, per_device(): repeated = jnp.tile(factor, (column.shape[0] // PANEL, 1))  15.1 us
  transfers between devices with their start and end apart: 2, of which 2 were waited for; matrix products, arithmetic and copies ran while one was open for 0% of the time, Pallas kernels for 0%

profile of v1, /device:TPU:0, one launch (start us, length us, event | category | flops | bytes accessed | tf_op | source)
XLA Modules:
  0.0 407.9 jit_solution(14835351549331162086)
XLA Ops:
  9.2 2.6 gather_fusion
  11.8 6.3 %all-to-all-start = ((bf16[8,64,440]{2,1,0:T(8,128)(2,1)}), bf16[8,64,440]{2,1,0:T(8,128)(2,1)S(1)}, u32[]{:S(2)}, u32[]{:S(2)}) async-start(bf16[8,64,440]{2,1,0:T(8,128)(2,1)} %bitcast.2), calls=%async_computation | async-start | bytes 1048576 | tf_op jit(solution)/shard_map/all_to_all | solution.py:54
  18.3 15.2 %all-to-all-done = bf16[8,64,440]{2,1,0:T(8,128)(2,1)S(1)} async-done(((bf16[8,64,440]{2,1,0:T(8,128)(2,1)}), bf16[8,64,440]{2,1,0:T(8,128)(2,1)S(1)}, u32[]{:S(2)}, u32[]{:S(2)}) %all-to-all-start) | async-done | bytes 450592 | tf_op jit(solution)/shard_map/all_to_all | solution.py:54
  35.8 27.8 %all-gather.3.cloned.1.call-done = bf16[2048,440]{1,0:T(8,128)(2,1)} async-done(((bf16[256,440]{1,0:T(8,128)(2,1)}), bf16[2048,440]{1,0:T(8,128)(2,1)}) %all-gather.3.cloned.1.call-update) | async-done | bytes 1802256 | tf_op jit(solution)/shard_map/all_gather | solution.py:66
  63.5 7.6 %gather_fusion.2 = bf16[1792,440]{1,0:T(8,128)(2,1)S(1)} fusion(bf16[2048,440]{1,0:T(8,128)(2,1)} %all-gather.3.cloned.1.call-done, s32[2048]{0:T(1024)S(1)} %pad_clamp_fusion), kind=kCustom, calls=%fused_computation.2 | custom fusion | bytes 3161088 | tf_op jit(solution)/shard_map/gather | solution.py:78
  73.7 3.0 select_add_fusion
  76.7 3.0 copy-done.12
  80.8 11.7 %cholesky.214 = f32[128,128]{1,0:T(8,128)S(1)} custom-call(f32[128,128]{1,0:T(8,128)S(1)} %cholesky.346), custom_call_target="Cholesky" | custom-call | tf_op jit(solution)/shard_map/jit(cholesky)/cholesky | solution.py:87
  92.6 9.8 %custom-call.17 = f32[1,128,128]{1,2,0:T(8,128)S(1)} custom-call(f32[1,128,128]{2,1,0:T(8,128)S(1)} %get-tuple-element.107), custom_call_target="InvertDiagBlocksLowerTriangular" | custom-call | tf_op jit(solution)/shard_map/jit(cholesky)/cholesky | solution.py:87
  102.9 11.9 %cholesky.231 = f32[128,128]{1,0:T(8,128)S(1)} custom-call(f32[128,128]{1,0:T(8,128)S(1)} %convolution_subtract_fusion.14), custom_call_target="Cholesky" | custom-call | tf_op jit(solution)/shard_map/jit(cholesky)/cholesky | solution.py:87
  116.9 4.0 while.8
  121.0 19.7 %custom-call.18 = f32[2,128,128]{1,2,0:T(8,128)S(1)} custom-call(f32[2,128,128]{2,1,0:T(8,128)S(1)} %get-tuple-element.30), custom_call_target="InvertDiagBlocksLowerTriangular" | custom-call | tf_op jit(solution)/shard_map/triangular_solve/custom-call.0 | solution.py:88
  140.6 2.1 fusion.13
  142.8 2.1 convolution_subtract_fusion.9
  144.9 1.9 fusion.44
  147.0 2.1 copy.45
  149.1 2.0 maximum_select_fusion
  151.1 3.3 convolution_subtract_fusion.5
  154.4 5.2 %convolution_subtract_fusion.4 = f32[1792,256]{0,1:T(8,128)} fusion(f32[1792,256]{0,1:T(8,128)S(1)} %maximum_select_fusion, f32[1792,1024]{0,1:T(8,128)} %copy-done.12), kind=kOutput, calls=%fused_computation.17 | convolution fusion | flops 1409744896 | bytes 5767168 | tf_op jit(solution)/shard_map/dot_general | solution.py:33
  159.6 4.5 %convolution_subtract_fusion.2 = f32[1792,256]{0,1:T(8,128)} fusion(f32[1792,256]{0,1:T(8,128)S(1)} %maximum_select_fusion, f32[1792,1024]{0,1:T(8,128)} %copy-done.12), kind=kOutput, calls=%fused_computation.15 | convolution fusion | flops 1409744896 | bytes 5767168 | tf_op jit(solution)/shard_map/dot_general | solution.py:33
  165.3 11.7 %cholesky.248 = f32[128,128]{1,0:T(8,128)S(1)} custom-call(f32[128,128]{1,0:T(8,128)S(1)} %cholesky.349), custom_call_target="Cholesky" | custom-call | tf_op jit(solution)/shard_map/jit(cholesky)/cholesky | solution.py:87
  177.7 9.8 %custom-call.19 = f32[1,128,128]{1,2,0:T(8,128)S(1)} custom-call(f32[1,128,128]{2,1,0:T(8,128)S(1)} %get-tuple-element.103), custom_call_target="InvertDiagBlocksLowerTriangular" | custom-call | tf_op jit(solution)/shard_map/jit(cholesky)/cholesky | solution.py:87
  188.2 11.7 %cholesky.265 = f32[128,128]{1,0:T(8,128)S(1)} custom-call(f32[128,128]{1,0:T(8,128)S(1)} %convolution_subtract_fusion.13), custom_call_target="Cholesky" | custom-call | tf_op jit(solution)/shard_map/jit(cholesky)/cholesky | solution.py:87
  201.9 4.0 while.9
  205.9 19.7 %custom-call.20 = f32[2,128,128]{1,2,0:T(8,128)S(1)} custom-call(f32[2,128,128]{2,1,0:T(8,128)S(1)} %get-tuple-element.31), custom_call_target="InvertDiagBlocksLowerTriangular" | custom-call | tf_op jit(solution)/shard_map/triangular_solve/custom-call.0 | solution.py:88
  225.6 2.2 fusion.11
  228.9 1.9 fusion.40
  232.1 3.0 copy.49
  235.1 2.1 maximum_select_fusion.1
  239.6 3.1 convolution_subtract_fusion.1
  243.9 11.7 %cholesky.282 = f32[128,128]{1,0:T(8,128)S(1)} custom-call(f32[128,128]{1,0:T(8,128)S(1)} %cholesky.352), custom_call_target="Cholesky" | custom-call | tf_op jit(solution)/shard_map/jit(cholesky)/cholesky | solution.py:87
  256.3 9.8 %custom-call.21 = f32[1,128,128]{1,2,0:T(8,128)S(1)} custom-call(f32[1,128,128]{2,1,0:T(8,128)S(1)} %get-tuple-element.99), custom_call_target="InvertDiagBlocksLowerTriangular" | custom-call | tf_op jit(solution)/shard_map/jit(cholesky)/cholesky | solution.py:87
  266.6 12.1 %cholesky.299 = f32[128,128]{1,0:T(8,128)S(1)} custom-call(f32[128,128]{1,0:T(8,128)S(1)} %convolution_subtract_fusion.12), custom_call_target="Cholesky" | custom-call | tf_op jit(solution)/shard_map/jit(cholesky)/cholesky | solution.py:87
  280.7 4.0 while.10
  284.7 19.7 %custom-call.22 = f32[2,128,128]{1,2,0:T(8,128)S(1)} custom-call(f32[2,128,128]{2,1,0:T(8,128)S(1)} %get-tuple-element.32), custom_call_target="InvertDiagBlocksLowerTriangular" | custom-call | tf_op jit(solution)/shard_map/triangular_solve/custom-call.0 | solution.py:88
  304.4 2.2 fusion.9
  311.0 2.9 copy.54
  313.9 2.1 maximum_select_fusion.2
  320.5 11.7 %cholesky.316 = f32[128,128]{1,0:T(8,128)S(1)} custom-call(f32[128,128]{1,0:T(8,128)S(1)} %cholesky.355), custom_call_target="Cholesky" | custom-call | tf_op jit(solution)/shard_map/jit(cholesky)/cholesky | solution.py:87
  332.9 9.8 %custom-call.23 = f32[1,128,128]{1,2,0:T(8,128)S(1)} custom-call(f32[1,128,128]{2,1,0:T(8,128)S(1)} %get-tuple-element.95), custom_call_target="InvertDiagBlocksLowerTriangular" | custom-call | tf_op jit(solution)/shard_map/jit(cholesky)/cholesky | solution.py:87
  343.2 11.9 %cholesky.333 = f32[128,128]{1,0:T(8,128)S(1)} custom-call(f32[128,128]{1,0:T(8,128)S(1)} %convolution_subtract_fusion.11), custom_call_target="Cholesky" | custom-call | tf_op jit(solution)/shard_map/jit(cholesky)/cholesky | solution.py:87
  357.2 4.0 while.11
  361.2 19.7 %custom-call.24 = f32[2,128,128]{1,2,0:T(8,128)S(1)} custom-call(f32[2,128,128]{2,1,0:T(8,128)S(1)} %get-tuple-element.33), custom_call_target="InvertDiagBlocksLowerTriangular" | custom-call | tf_op jit(solution)/shard_map/triangular_solve/custom-call.0 | solution.py:88
  380.9 2.2 fusion.7
  384.1 1.9 fusion.32
  387.4 2.7 copy.60
  390.2 2.1 maximum_select_fusion.3
  394.8 3.5 fusion
  (159 shorter events, 54.2 us)
Async XLA Ops:
  9.2 9.0 %copy-start.16 = (s32[8,1]{0,1:T(1,128)S(1)}, s32[8,1]{0,1:T(1,128)}, u32[]{:S(2)}) copy-start(s32[8,1]{0,1:T(1,128)} %param.10) | copy-start | bytes 100
  9.2 9.0 %copy-start.17 = (s32[8,1]{0,1:T(1,128)S(1)}, s32[8,1]{0,1:T(1,128)}, u32[]{:S(2)}) copy-start(s32[8,1]{0,1:T(1,128)} %param.9) | copy-start | bytes 100
  11.8 21.7 %all-to-all-start = ((bf16[8,64,440]{2,1,0:T(8,128)(2,1)}), bf16[8,64,440]{2,1,0:T(8,128)(2,1)S(1)}, u32[]{:S(2)}, u32[]{:S(2)}) async-start(bf16[8,64,440]{2,1,0:T(8,128)(2,1)} %bitcast.2), calls=%async_computation | async-start | bytes 1048576 | tf_op jit(solution)/shard_map/all_to_all | solution.py:54
  18.1 45.4 %all-gather.3.cloned.1.call-start = ((), (), s32[]{:S(2)}) async-start(), calls=%async_computation.1 | async-start | bytes 2359296 | tf_op jit(solution)/shard_map/all_gather | solution.py:66
  71.2 2.6 copy-start.5
  71.2 2.3 copy-start
  76.7 3.0 copy-start.12
  154.4 9.8 %copy-start.8 = (f32[1792,256]{0,1:T(8,128)}, f32[1792,256]{0,1:T(8,128)S(1)}, u32[]{:S(2)}) copy-start(f32[1792,256]{0,1:T(8,128)S(1)} %convolution_subtract_fusion.5) | copy-start | bytes 5505028
  225.6 2.3 copy-start.9
  235.1 2.3 copy-start.14
  237.4 1.9 copy-start.1
  237.4 2.2 copy-start.13
  239.6 3.1 copy-start.10
  304.4 2.3 copy-start.11
  313.9 2.3 copy-start.15
  316.2 1.9 copy-start.3
  318.1 1.3 copy-start.6
  380.9 2.3 copy-start.7
  390.2 2.3 copy-start.2
  390.2 2.9 copy-start.4
Sparse Core Ops, SparseCore 0:
  35.5 27.9 all-gather.2
